TPU v7x, 32 devices: a whole 2x2x4 slice. The times are simulated.
32 devices in a mesh: dp: 2 (over y), expert: 16 (over z, x, core).
Axes of the slice: x: 2, y: 2, z: 4, core: 2. Of those that a mesh axis runs over, the one named last changes fastest.
Arguments:
- attention: bfloat16 [16, 2, 16, 1024], P('expert', 'dp'), may hold values from -6 to 6
- residual: bfloat16 [16, 2, 16, 2048], P('expert', 'dp')
- out_proj: bfloat16 [1024, 2048], P(None, 'dp'), may hold values from -0.1875 to 0.1875
- gain_in: float32 [2048], replicated, may hold values from 0.5 to 1.5
- router: bfloat16 [2048, 16], P(None, 'dp')
- expert_ids: int32 [16, 2, 16, 6], P('expert'), may hold values from 0 to 15, all different within a row; in each aligned block of 16 rows (0 to 15, 16 to 31, ..., all dimensions but the last counted through in order) at most 12 rows name the same one
- live_rows: int32 [2, 16], P(None, 'expert'), may hold values from 1 to 16, 224 in all within a row
- expert_gate: bfloat16 [16, 1408, 2048], P('expert', 'dp'), may hold values from -0.25 to 0.25
- expert_up: bfloat16 [16, 1408, 2048], P('expert', 'dp'), may hold values from -0.25 to 0.25
- expert_down: bfloat16 [16, 1408, 2048], P('expert', None, 'dp'), may hold values from -0.15625 to 0.15625
- shared_gate: bfloat16 [1408, 2048], P('dp'), may hold values from -0.125 to 0.125
- shared_up: bfloat16 [1408, 2048], P('dp'), may hold values from -0.125 to 0.125
- shared_down: bfloat16 [1408, 2048], P(None, 'dp'), may hold values from -0.15625 to 0.15625
- gain_out: float32 [2048], replicated, may hold values from 0.5 to 1.5
Outputs:
- stream: bfloat16 [16, 2, 16, 2048], P('expert', 'dp')
- normed: bfloat16 [16, 2, 16, 2048], P('expert', 'dp')
Inputs may be any that keep to these rules, and one draw needn't show every extreme that they name: `expert_ids`: each row names 6 different experts; the 16 rows of one block [o, g] name one expert at most 12 times, a bound that some block reaches. The live rows of a device are its first live_rows[g, o]; the 16 counts of each g sum to 224, and one of them is 16.
All inputs are finite; a program needn't handle non-finite values.
Results may differ from a plain program's by a relative error of at most 0.0095.
Values may be sent and summed in bfloat16 or wider, within the bound.
No kernel may reach another device: no remote copies, remote signals or barrier semaphores. Data moves between devices by JAX's collectives and lax.ppermute only.
A program may use at most 128 MiB of HBM per device.

v0:
```python
import jax
import jax.numpy as jnp
from jax import lax
from jax.sharding import PartitionSpec as P


def rms_scale(features, scale_gain):
    return (
        features
        * lax.rsqrt(jnp.mean(features * features, axis=-1, keepdims=True) + 1e-06)
        * scale_gain
    )


def by_rows(left, weight_rows):
    return lax.dot_general(
        left, weight_rows, (((1,), (1,)), ((), ())), preferred_element_type=jnp.float32
    )


def gather_axis(x, name, axis):
    n = lax.axis_size(name)
    if n == 1:
        return x
    me = lax.axis_index(name)
    pieces = [x]
    for shift in range(1, n):
        pieces.append(lax.ppermute(x, name, [(j, (j + shift) % n) for j in range(n)]))
    if n == 2:
        first = jnp.where(me == 0, pieces[0], pieces[1])
        second = jnp.where(me == 0, pieces[1], pieces[0])
        ordered = [first, second]
        return jnp.concatenate(ordered, axis=axis)
    stacked = jnp.stack(pieces, 0)
    order = (me - jnp.arange(n)) % n
    ordered = jnp.take(stacked, order, axis=0)
    ordered = jnp.moveaxis(ordered, 0, axis)
    shape = list(x.shape)
    shape[axis] = shape[axis] * n
    return ordered.reshape(shape)


def shards(
    attention,
    residual,
    out_proj,
    gain_in,
    router,
    expert_ids,
    live_rows,
    expert_gate,
    expert_up,
    expert_down,
    shared_gate,
    shared_up,
    shared_down,
    gain_out,
):
    groups = lax.axis_size("dp")
    experts = lax.axis_size("expert")
    row_count = attention.shape[2]
    feature_width = residual.shape[3]
    top_count = expert_ids.shape[3]
    capacity = max(2, (2 * row_count * top_count + experts - 1) // experts)
    gate_local = expert_gate[0]
    up_local = expert_up[0]
    down_local = expert_down[0]
    column_width = down_local.shape[1]
    rows_all = groups * row_count
    pieces = gather_axis(attention, "dp", 1)
    flattened = pieces.reshape(-1, pieces.shape[-1])
    product = jnp.dot(flattened, out_proj, preferred_element_type=jnp.float32).astype(jnp.bfloat16)
    columns = product.reshape(pieces.shape[:-1] + (out_proj.shape[1],))
    projected = lax.all_to_all(columns, "dp", split_axis=1, concat_axis=3, tiled=True)[0, 0]
    stream_in = residual[0, 0].astype(jnp.float32) + projected.astype(jnp.float32)
    normal_rows = rms_scale(stream_in, gain_in).astype(jnp.bfloat16)
    column = gather_axis(normal_rows, "dp", 0)
    logit_part = jnp.dot(column, router, preferred_element_type=jnp.float32)
    logits = gather_axis(logit_part, "dp", 1)
    flat_experts = expert_ids[0].reshape(rows_all, top_count)
    picked = jnp.take_along_axis(logits, flat_experts, axis=1)
    probabilities = jax.nn.softmax(picked, axis=1)
    row_live = (jnp.arange(row_count, dtype=jnp.int32)[None, :] < live_rows[:, 0][:, None]).reshape(
        rows_all
    )
    slot_live = jnp.broadcast_to(row_live[:, None], (rows_all, top_count))
    weights = probabilities.astype(jnp.bfloat16) * slot_live.astype(jnp.bfloat16)
    block_experts = flat_experts.reshape(groups, row_count * top_count)
    block_live = slot_live.reshape(groups, row_count * top_count)
    onehot = (
        (block_experts[:, :, None] == jnp.arange(experts, dtype=jnp.int32)) & block_live[:, :, None]
    ).astype(jnp.int32)
    before = jnp.cumsum(onehot, axis=1) - onehot
    position = jnp.sum(before * onehot, axis=2)
    slot_total = experts * groups * capacity
    offsets = jnp.arange(groups, dtype=jnp.int32)[:, None] * capacity
    target = jnp.where(
        block_live, block_experts * (groups * capacity) + offsets + position, slot_total
    ).reshape(rows_all, top_count)
    slot_hit = target[:, :, None] == jnp.arange(slot_total, dtype=jnp.int32)[None, None, :]
    fill = jnp.any(slot_hit, axis=1).astype(jnp.bfloat16)
    outgoing = (
        lax.dot_general(fill, column, (((0,), (0,)), ((), ())), preferred_element_type=jnp.float32)
        .astype(jnp.bfloat16)
        .reshape(experts, groups * capacity, feature_width)
    )
    slot_rows = lax.all_to_all(outgoing, "expert", split_axis=0, concat_axis=0, tiled=True)
    flattened = slot_rows.reshape(-1, slot_rows.shape[-1])
    gate_value = by_rows(flattened, gate_local)
    up_value = by_rows(flattened, up_local)
    hidden = (jax.nn.silu(gate_value) * up_value).astype(jnp.bfloat16)
    shared_gate_value = by_rows(column, shared_gate)
    shared_up_value = by_rows(column, shared_up)
    shared_hidden = (jax.nn.silu(shared_gate_value) * shared_up_value).astype(jnp.bfloat16)
    routed_piece = gather_axis(hidden, "dp", 1)
    shared_piece = gather_axis(shared_hidden, "dp", 1)
    routed_total = jnp.dot(routed_piece, down_local, preferred_element_type=jnp.float32)
    shared = jnp.dot(shared_piece, shared_down, preferred_element_type=jnp.float32)
    expert_out = routed_total.astype(jnp.bfloat16).reshape(experts, groups * capacity, column_width)
    returned = lax.all_to_all(
        expert_out, "expert", split_axis=0, concat_axis=0, tiled=True
    ).reshape(slot_total, column_width)
    combine = jnp.sum(
        jnp.where(slot_hit, weights[:, :, None], jnp.zeros((), jnp.bfloat16)), axis=1
    ).astype(jnp.bfloat16)
    routed = jnp.dot(combine, returned, preferred_element_type=jnp.float32)
    combined = jnp.where(row_live[:, None], routed + shared, 0.0).reshape(
        groups, row_count, column_width
    )
    summed = lax.all_to_all(combined, "dp", split_axis=0, concat_axis=2, tiled=True)[0]
    stream_sum = stream_in + summed
    stream = stream_sum.astype(jnp.bfloat16)[None, None]
    normed = rms_scale(stream_sum, gain_out).astype(jnp.bfloat16)[None, None]
    return (stream, normed)


def solution(mesh):
    placed = (
        P("expert", "dp", None, None),
        P("expert", "dp", None, None),
        P(None, "dp"),
        P(),
        P(None, "dp"),
        P("expert", None, None, None),
        P(None, "expert"),
        P("expert", "dp", None),
        P("expert", "dp", None),
        P("expert", None, "dp"),
        P("dp", None),
        P("dp", None),
        P(None, "dp"),
        P(),
    )
    return jax.shard_map(
        shards,
        mesh=mesh,
        in_specs=placed,
        out_specs=(P("expert", "dp", None, None), P("expert", "dp", None, None)),
        check_vma=False,
    )
```

profile of v0, /device:TPU:0, one launch (start us, length us, event | category | flops | bytes accessed | tf_op | source)
XLA Modules:
  0.0 128.7 jit_solution(17526194311899023386)
XLA Ops:
  0.7 3.0 %collective-permute-start = (bf16[1,1,16,1024]{3,2,1,0:T(8,128)(2,1)}, bf16[1,1,16,1024]{3,2,1,0:T(8,128)(2,1)S(1)}, u32[]{:S(2)}, u32[]{:S(2)}) collective-permute-start(bf16[1,1,16,1024]{3,2,1,0:T(8,128)(2,1)} %param.14), channel_id=1, source_target_pairs={{0,16},{16,0},{1,17},{17,1},{2,18},{18,2},{3,19},{19,3},{4,20},{20... | collective-permute-start | bytes 98312 | tf_op jit(solution)/shard_map/ppermute | solution.py:28
  3.7 0.8 copy.70
  4.6 0.7 iota_compare_fusion.2
  6.1 0.8 reshape_reshape_squeeze.5
  7.1 0.8 broadcast_select_fusion.7
  7.9 2.7 %convolution_convert_fusion.1 = bf16[32,1024]{1,0:T(8,128)(2,1)} fusion(bf16[32,1024]{1,0:T(8,128)(2,1)S(1)} %bitcast.92, bf16[1024,1024]{1,0:T(8,128)(2,1)} %param.16), kind=kOutput, calls=%fused_computation.13 | convolution fusion | flops 67141632 | bytes 2228224 | tf_op jit(solution)/shard_map/dot_general | solution.py:72
  10.6 3.3 %all-to-all-start = ((bf16[1,2,16,1024]{3,2,0,1:T(8,128)(2,1)}), bf16[1,2,16,1024]{3,2,0,1:T(8,128)(2,1)S(1)}, u32[]{:S(2)}, u32[]{:S(2)}) async-start(bf16[1,2,16,1024]{3,2,0,1:T(8,128)(2,1)} %bitcast.2), calls=%async_computation | async-start | bytes 131072 | tf_op jit(solution)/shard_map/all_to_all | solution.py:74
  14.0 4.1 %all-to-all-done = bf16[1,2,16,1024]{3,2,0,1:T(8,128)(2,1)S(1)} async-done(((bf16[1,2,16,1024]{3,2,0,1:T(8,128)(2,1)}), bf16[1,2,16,1024]{3,2,0,1:T(8,128)(2,1)S(1)}, u32[]{:S(2)}, u32[]{:S(2)}) %all-to-all-start) | async-done | bytes 65568 | tf_op jit(solution)/shard_map/all_to_all | solution.py:74
  18.6 4.1 %collective-permute-done.1 = bf16[16,2048]{1,0:T(8,128)(2,1)S(1)} collective-permute-done((bf16[16,2048]{1,0:T(8,128)(2,1)S(1)}, bf16[16,2048]{1,0:T(8,128)(2,1)S(1)}, u32[]{:S(2)}, u32[]{:S(2)}) %collective-permute-start.1) | collective-permute-done | bytes 65568 | tf_op jit(solution)/shard_map/ppermute | solution.py:28
  22.8 0.6 convolution_convert_fusion
  23.4 41.9 %all_to_all.34 = bf16[16,24,2048]{2,1,0:T(8,128)(2,1)S(1)} all-to-all(bf16[16,24,2048]{2,1,0:T(8,128)(2,1)S(1)} %bitcast.83), channel_id=1, replica_groups=mesh['dp'=2,'expert'=16] {'expert'}, dimensions={0} | all-to-all | bytes 3145728 | tf_op jit(solution)/shard_map/all_to_all | solution.py:107
  65.3 1.7 %fusion.4 = f32[384,704]{0,1:T(8,128)S(1)} fusion(bf16[384,2048]{1,0:T(8,128)(2,1)S(1)} %bitcast.84, bf16[1,704,2048]{2,1,0:T(8,128)(2,1)S(1)} %copy-done.4), kind=kOutput, calls=%fused_computation.5 | convolution fusion | flops 1107296256 | bytes 5537792 | tf_op jit(solution)/shard_map/dot_general | solution.py:16
  67.2 2.5 %fusion.12 = bf16[384,704]{0,1:T(8,128)(2,1)} fusion(bf16[384,2048]{1,0:T(8,128)(2,1)S(1)} %bitcast.85, bf16[1,704,2048]{2,1,0:T(8,128)(2,1)S(1)} %copy-done.5, f32[384,704]{0,1:T(8,128)S(1)} %fusion.4), kind=kOutput, calls=%fused_computation.10 | convolution fusion | flops 1108918272 | bytes 6078464 | tf_op jit(solution)/shard_map/dot_general | solution.py:16
  70.0 2.7 %fusion.39 = f32[32,704]{1,0:T(8,128)S(1)} fusion(bf16[704,2048]{1,0:T(8,128)(2,1)} %param.24, bf16[16,2048]{1,0:T(8,128)(2,1)S(1)} %get-tuple-element.9, bf16[16,2048]{1,0:T(8,128)(2,1)S(1)} %get-tuple-element.8), kind=kOutput, calls=%fused_computation.73 | convolution fusion | flops 92536832 | bytes 3104768 | tf_op jit(solution)/shard_map/dot_general | solution.py:16
  72.7 12.2 %collective-permute-done.3 = bf16[384,704]{0,1:T(8,128)(2,1)} collective-permute-done((bf16[384,704]{0,1:T(8,128)(2,1)}, bf16[384,704]{0,1:T(8,128)(2,1)}, u32[]{:S(2)}, u32[]{:S(2)}) %collective-permute-start.3) | collective-permute-done | bytes 540704 | tf_op jit(solution)/shard_map/ppermute | solution.py:28
  84.9 1.3 %broadcast_select_fusion.1 = (bf16[384,704]{0,1:T(8,128)(2,1)S(1)}, bf16[384,704]{0,1:T(8,128)(2,1)S(1)}) fusion(bf16[384,704]{0,1:T(8,128)(2,1)} %fusion.12, bf16[384,704]{0,1:T(8,128)(2,1)} %collective-permute-done.3, pred[]{:T(512)S(6)} %eq.16), kind=kLoop, calls=%fused_computation.18 | loop fusion | flops 540672 | bytes 2162689 | tf_op jit(solution)/shard_map/jit(_where)/select_n | solution.py:30
  86.3 2.3 %fusion.6 = bf16[384,1024]{1,0:T(8,128)(2,1)} fusion(bf16[1,1408,1024]{2,1,0:T(8,128)(2,1)S(1)} %copy-done, bf16[384,704]{0,1:T(8,128)(2,1)S(1)} %get-tuple-element.3, bf16[384,704]{0,1:T(8,128)(2,1)S(1)} %get-tuple-element.2), kind=kOutput, calls=%fused_computation.8 | convolution fusion | flops 1109852160 | bytes 4751360 | tf_op jit(solution)/shard_map/dot_general | solution.py:117
  88.6 4.6 %all-to-all-start.2 = ((bf16[16,24,1024]{2,1,0:T(8,128)(2,1)}), bf16[16,24,1024]{2,1,0:T(8,128)(2,1)}, u32[]{:S(2)}, u32[]{:S(2)}) async-start(bf16[16,24,1024]{2,1,0:T(8,128)(2,1)} %bitcast.90), calls=%async_computation.2 | async-start | bytes 1572864 | tf_op jit(solution)/shard_map/all_to_all | solution.py:120
  93.4 0.3 collective-permute-start.2
  93.7 2.7 %multiply_convert_fusion.2 = bf16[32,704]{1,0:T(8,128)(2,1)S(1)} fusion(f32[32,704]{1,0:T(8,128)S(1)} %fusion.39, bf16[704,2048]{1,0:T(8,128)(2,1)} %param.25, bf16[16,2048]{1,0:T(8,128)(2,1)S(1)} %get-tuple-element.9, bf16[16,2048]{1,0:T(8,128)(2,1)S(1)} %get-tuple-element.8), kind=kOutput, calls=%fused_computation.35 | convolution fusion | flops 92672000 | bytes 3149824 | tf_op jit(solution)/shard_map/dot_general | solution.py:16
  96.4 1.8 %collective-permute-start.4 = (bf16[32,704]{1,0:T(8,128)(2,1)S(1)}, bf16[32,704]{1,0:T(8,128)(2,1)S(1)}, u32[]{:S(2)}, u32[]{:S(2)}) collective-permute-start(bf16[32,704]{1,0:T(8,128)(2,1)S(1)} %multiply_convert_fusion.2), channel_id=1, source_target_pairs={{0,16},{16,0},{1,17},{17,1},{2,18},{18,2},{3,19},{19,3},{4,20},{20... | collective-permute-start | bytes 135176 | tf_op jit(solution)/shard_map/ppermute | solution.py:28
  98.2 1.7 %gather_fusion = f32[192]{0:T(256)S(1)} fusion(f32[32,16]{0,1:T(8,128)S(1)} %pad_maximum_fusion.2, s32[192]{0:T(256)S(1)} %reshape.303), kind=kCustom, calls=%fused_computation | custom fusion | bytes 3072 | tf_op jit(solution)/shard_map/jit(take_along_axis)/gather | solution.py:81
  100.8 11.2 %all-to-all-done.2 = bf16[16,24,1024]{2,1,0:T(8,128)(2,1)} async-done(((bf16[16,24,1024]{2,1,0:T(8,128)(2,1)}), bf16[16,24,1024]{2,1,0:T(8,128)(2,1)}, u32[]{:S(2)}, u32[]{:S(2)}) %all-to-all-start.2) | async-done | bytes 786464 | tf_op jit(solution)/shard_map/all_to_all | solution.py:120
  112.0 1.4 %fusion.42 = f32[32,1024]{1,0:T(8,128)S(1)} fusion(bf16[32,384]{1,0:T(8,128)(2,1)S(1)} %fusion.21, bf16[384,1024]{1,0:T(8,128)(2,1)} %bitcast.14), kind=kOutput, calls=%fused_computation.76 | convolution fusion | flops 25165824 | bytes 942080 | tf_op jit(solution)/shard_map/dot_general | solution.py:126
  113.3 3.1 %fusion.15 = f32[32,1024]{1,0:T(8,128)} fusion(f32[32,1024]{1,0:T(8,128)S(1)} %fusion.42, bf16[1408,1024]{1,0:T(8,128)(2,1)} %param.26, bf16[32,704]{1,0:T(8,128)(2,1)S(1)} %get-tuple-element.11, bf16[32,704]{1,0:T(8,128)(2,1)S(1)} %get-tuple-element.10, pred[32]{0:T(512)(128)(4,1)S(1)} %lt.57), kind=kOutput, calls=%fused_computation.12 | convolution fusion | flops 92520448 | bytes 3235872 | tf_op jit(solution)/shard_map/dot_general | solution.py:118
  116.4 3.4 %all-to-all-start.3 = ((f32[2,16,1024]{2,1,0:T(8,128)}), f32[2,16,1024]{2,1,0:T(8,128)S(1)}, u32[]{:S(2)}, u32[]{:S(2)}) async-start(f32[2,16,1024]{2,1,0:T(8,128)} %bitcast.15), calls=%async_computation.3 | async-start | bytes 262144 | tf_op jit(solution)/shard_map/all_to_all | solution.py:130
  120.1 0.7 convert.13
  120.7 3.5 %all-to-all-done.3 = f32[2,16,1024]{2,1,0:T(8,128)S(1)} async-done(((f32[2,16,1024]{2,1,0:T(8,128)}), f32[2,16,1024]{2,1,0:T(8,128)S(1)}, u32[]{:S(2)}, u32[]{:S(2)}) %all-to-all-start.3) | async-done | bytes 131104 | tf_op jit(solution)/shard_map/all_to_all | solution.py:130
  124.3 0.8 copy.88
  125.0 1.0 squeeze.17
  126.1 1.2 fusion.24
  127.2 1.4 %multiply_convert_fusion = (bf16[1,1,16,2048]{3,2,1,0:T(8,128)(2,1)}, bf16[1,1,16,2048]{3,2,1,0:T(8,128)(2,1)}) fusion(f32[2048]{0:T(1024)} %param.27, f32[16]{0:T(128)S(1)} %add_rsqrt_fusion, f32[1,1,16,2048]{3,2,1,0:T(8,128)S(1)} %squeeze.17, f32[1,1,16,2048]{3,2,1,0:T(8,128)S(1)} %reshape.295, bf16[1,1,16,2048]{3,2,1,0:T(8,128)(2,1)S(1)} %copy-done.1), kind=kLoop, calls=%fused_computation.30 | loop fusion | flops 229376 | bytes 467008 | tf_op jit(solution)/shard_map/convert_element_type | solution.py:133
  (61 shorter events, 3.5 us)
Async XLA Ops:
  0.6 85.6 %copy-start = (bf16[1,1408,1024]{2,1,0:T(8,128)(2,1)S(1)}, bf16[1,1408,1024]{2,1,0:T(8,128)(2,1)}, u32[]{:S(2)}) copy-start(bf16[1,1408,1024]{2,1,0:T(8,128)(2,1)} %param.23) | copy-start | bytes 8650756
  0.6 17.5 %copy-start.1 = (bf16[1,1,16,2048]{3,2,1,0:T(8,128)(2,1)S(1)}, bf16[1,1,16,2048]{3,2,1,0:T(8,128)(2,1)}, u32[]{:S(2)}) copy-start(bf16[1,1,16,2048]{3,2,1,0:T(8,128)(2,1)} %param.15) | copy-start | bytes 196612
  0.7 17.7 %copy-start.3 = (f32[2048]{0:T(1024)S(1)}, f32[2048]{0:T(1024)}, u32[]{:S(2)}) copy-start(f32[2048]{0:T(1024)} %param.17) | copy-start | bytes 24580
  0.7 6.5 %collective-permute-start = (bf16[1,1,16,1024]{3,2,1,0:T(8,128)(2,1)}, bf16[1,1,16,1024]{3,2,1,0:T(8,128)(2,1)S(1)}, u32[]{:S(2)}, u32[]{:S(2)}) collective-permute-start(bf16[1,1,16,1024]{3,2,1,0:T(8,128)(2,1)} %param.14), channel_id=1, source_target_pairs={{0,16},{16,0},{1,17},{17,1},{2,18},{18,2},{3,19},{19,3},{4,20},{20... | collective-permute-start | bytes 98312 | tf_op jit(solution)/shard_map/ppermute | solution.py:28
  10.6 7.4 %all-to-all-start = ((bf16[1,2,16,1024]{3,2,0,1:T(8,128)(2,1)}), bf16[1,2,16,1024]{3,2,0,1:T(8,128)(2,1)S(1)}, u32[]{:S(2)}, u32[]{:S(2)}) async-start(bf16[1,2,16,1024]{3,2,0,1:T(8,128)(2,1)} %bitcast.2), calls=%async_computation | async-start | bytes 131072 | tf_op jit(solution)/shard_map/all_to_all | solution.py:74
  18.4 4.3 %collective-permute-start.1 = (bf16[16,2048]{1,0:T(8,128)(2,1)S(1)}, bf16[16,2048]{1,0:T(8,128)(2,1)S(1)}, u32[]{:S(2)}, u32[]{:S(2)}) collective-permute-start(bf16[16,2048]{1,0:T(8,128)(2,1)S(1)} %multiply_convert_fusion.1), channel_id=1, source_target_pairs={{0,16},{16,0},{1,17},{17,1},{2,18},{18,2},{3,19},{19,3},{4,20},{20... | collective-permute-start | bytes 196616 | tf_op jit(solution)/shard_map/ppermute | solution.py:28
  22.8 42.6 %copy-start.4 = (bf16[1,704,2048]{2,1,0:T(8,128)(2,1)S(1)}, bf16[1,704,2048]{2,1,0:T(8,128)(2,1)}, u32[]{:S(2)}) copy-start(bf16[1,704,2048]{2,1,0:T(8,128)(2,1)} %param.21) | copy-start | bytes 8650756
  65.3 1.8 %copy-start.5 = (bf16[1,704,2048]{2,1,0:T(8,128)(2,1)S(1)}, bf16[1,704,2048]{2,1,0:T(8,128)(2,1)}, u32[]{:S(2)}) copy-start(bf16[1,704,2048]{2,1,0:T(8,128)(2,1)} %param.22) | copy-start | bytes 8650756
  67.2 2.5 %copy-start.2 = (s32[1,2,16,6]{2,1,3,0:T(2,128)S(1)}, s32[1,2,16,6]{2,1,3,0:T(2,128)}, u32[]{:S(2)}) copy-start(s32[1,2,16,6]{2,1,3,0:T(2,128)} %param.19) | copy-start | bytes 2308
  69.7 15.3 %collective-permute-start.3 = (bf16[384,704]{0,1:T(8,128)(2,1)}, bf16[384,704]{0,1:T(8,128)(2,1)}, u32[]{:S(2)}, u32[]{:S(2)}) collective-permute-start(bf16[384,704]{0,1:T(8,128)(2,1)} %fusion.12), channel_id=1, source_target_pairs={{0,16},{16,0},{1,17},{17,1},{2,18},{18,2},{3,19},{19,3},{4,20},{20... | collective-permute-start | bytes 1622024 | tf_op jit(solution)/shard_map/ppermute | solution.py:28
  86.2 7.0 %copy-start.6 = (bf16[2048,8]{0,1:T(8,128)(2,1)S(1)}, bf16[2048,8]{0,1:T(8,128)(2,1)}, u32[]{:S(2)}) copy-start(bf16[2048,8]{0,1:T(8,128)(2,1)} %param.18) | copy-start | bytes 98308
  88.6 23.4 %all-to-all-start.2 = ((bf16[16,24,1024]{2,1,0:T(8,128)(2,1)}), bf16[16,24,1024]{2,1,0:T(8,128)(2,1)}, u32[]{:S(2)}, u32[]{:S(2)}) async-start(bf16[16,24,1024]{2,1,0:T(8,128)(2,1)} %bitcast.90), calls=%async_computation.2 | async-start | bytes 1572864 | tf_op jit(solution)/shard_map/all_to_all | solution.py:120
  93.4 4.9 %collective-permute-start.2 = (f32[32,8]{0,1:T(8,128)S(1)}, f32[32,8]{0,1:T(8,128)S(1)}, u32[]{:S(2)}, u32[]{:S(2)}) collective-permute-start(f32[32,8]{0,1:T(8,128)S(1)} %fusion.40), channel_id=1, source_target_pairs={{0,16},{16,0},{1,17},{17,1},{2,18},{18,2},{3,19},{19,3},{4,20},{20... | collective-permute-start | bytes 3080 | tf_op jit(solution)/shard_map/ppermute | solution.py:28
  96.4 4.4 %collective-permute-start.4 = (bf16[32,704]{1,0:T(8,128)(2,1)S(1)}, bf16[32,704]{1,0:T(8,128)(2,1)S(1)}, u32[]{:S(2)}, u32[]{:S(2)}) collective-permute-start(bf16[32,704]{1,0:T(8,128)(2,1)S(1)} %multiply_convert_fusion.2), channel_id=1, source_target_pairs={{0,16},{16,0},{1,17},{17,1},{2,18},{18,2},{3,19},{19,3},{4,20},{20... | collective-permute-start | bytes 135176 | tf_op jit(solution)/shard_map/ppermute | solution.py:28
  116.4 7.8 %all-to-all-start.3 = ((f32[2,16,1024]{2,1,0:T(8,128)}), f32[2,16,1024]{2,1,0:T(8,128)S(1)}, u32[]{:S(2)}, u32[]{:S(2)}) async-start(f32[2,16,1024]{2,1,0:T(8,128)} %bitcast.15), calls=%async_computation.3 | async-start | bytes 262144 | tf_op jit(solution)/shard_map/all_to_all | solution.py:130
where the time goes:
time: 130 us; the launch traced here: 129 us
  blocking collectives  41.9 us (32%)
  waiting for transfers between devices  35.2 us (27%)
  matrix products  19.9 us (15%)
  starting transfers between devices  16.5 us (13%)
  other arithmetic  7.4 us (6%)
  local copies, waits for them, and re-layouts  6.88 us (5%)
    all_to_all x1, blocking collectives, shards(): lax.all_to_all(outgoing, 'expert', split_axis=0, concat_axis=0, tiled=True)  41.9 us
    ppermute x5, waiting for transfers between devices, gather_axis(): lax.ppermute(x, name, [(j, (j + shift) % n) for j in range(n)])  16.4 us
    all_to_all x1, waiting for transfers between devices, shards(): lax.all_to_all(expert_out, 'expert', split_axis=0, concat_axis=0, tiled=T...  11.2 us
    dot_general x4, matrix products, by_rows(): lax.dot_general(left, weight_rows, (((1,), (1,)), ((), ())), preferred_el...  9.61 us
    ppermute x5, starting transfers between devices, gather_axis(): lax.ppermute(x, name, [(j, (j + shift) % n) for j in range(n)])  5.24 us
    all_to_all x1, starting transfers between devices, shards(): lax.all_to_all(expert_out, 'expert', split_axis=0, concat_axis=0, tiled=T...  4.61 us
    all_to_all x1, waiting for transfers between devices, shards(): lax.all_to_all(columns, 'dp', split_axis=1, concat_axis=3, tiled=True)[0, 0]  4.09 us
    all_to_all x1, waiting for transfers between devices, shards(): lax.all_to_all(combined, 'dp', split_axis=0, concat_axis=2, tiled=True)[0]  3.53 us
  transfers between devices with their start and end apart: 8, of which 5 were waited for; matrix products, arithmetic and copies ran while one was open for 10% of the time, Pallas kernels for 0%

commit v1 on v0

--- a/solution.py
+++ b/solution.py
@@ -71,7 +71,9 @@
     flattened = pieces.reshape(-1, pieces.shape[-1])
     product = jnp.dot(flattened, out_proj, preferred_element_type=jnp.float32).astype(jnp.bfloat16)
     columns = product.reshape(pieces.shape[:-1] + (out_proj.shape[1],))
-    projected = lax.all_to_all(columns, "dp", split_axis=1, concat_axis=3, tiled=True)[0, 0]
+    projected = jnp.concatenate(
+        lax.all_to_all(jnp.stack(jnp.split(columns, lax.axis_size("dp"), 1)), "dp", 0, 0), 3
+    )[0, 0]
     stream_in = residual[0, 0].astype(jnp.float32) + projected.astype(jnp.float32)
     normal_rows = rms_scale(stream_in, gain_in).astype(jnp.bfloat16)
     column = gather_axis(normal_rows, "dp", 0)

time: 130 us -> 127 us (0.977)
  matrix products: 19.9 us -> 17.6 us
  waiting for transfers between devices: 35.2 us -> 37.4 us
  other arithmetic: 7.4 us -> 5.66 us
    ppermute x5, waiting for transfers between devices: 16.4 us -> 18.2 us  [gather_axis(): lax.ppermute(x, name, [(j, (j + shift) % n) for j in range(n)])]
    dot_general x4, matrix products: 9.61 us -> 7.97 us  [by_rows(): lax.dot_general(left, weight_rows, (((1,), (1,)), ((), ())), preferred_el...]
  transfers between devices with their start and end apart: 8 -> 8, of which waited for: 5 -> 6; matrix products, arithmetic and copies ran while one was open for 10% -> 11% of each run, Pallas kernels for 0% -> 0%
where the time goes in v1:
time: 127 us; the launch traced here: 126 us
  blocking collectives  41.9 us (33%)
  waiting for transfers between devices  37.4 us (29%)
  matrix products  17.6 us (14%)
  starting transfers between devices  16.8 us (13%)
  local copies, waits for them, and re-layouts  5.89 us (5%)
  other arithmetic  5.66 us (4%)
    all_to_all x1, blocking collectives, shards(): lax.all_to_all(outgoing, 'expert', split_axis=0, concat_axis=0, tiled=True)  41.9 us
    ppermute x5, waiting for transfers between devices, gather_axis(): lax.ppermute(x, name, [(j, (j + shift) % n) for j in range(n)])  18.2 us
    all_to_all x1, waiting for transfers between devices, shards(): lax.all_to_all(expert_out, 'expert', split_axis=0, concat_axis=0, tiled=T...  10.8 us
    dot_general x4, matrix products, by_rows(): lax.dot_general(left, weight_rows, (((1,), (1,)), ((), ())), preferred_el...  7.97 us
    ppermute x5, starting transfers between devices, gather_axis(): lax.ppermute(x, name, [(j, (j + shift) % n) for j in range(n)])  5.5 us
    all_to_all x1, starting transfers between devices, shards(): lax.all_to_all(expert_out, 'expert', split_axis=0, concat_axis=0, tiled=T...  4.6 us
    all_to_all x1, waiting for transfers between devices, shards(): lax.all_to_all(combined, 'dp', split_axis=0, concat_axis=2, tiled=True)[0]  4.3 us
    all_to_all x1, waiting for transfers between devices, shards(): lax.all_to_all(jnp.stack(jnp.split(columns, lax.axis_size('dp'), 1)), 'dp...  4.09 us
  transfers between devices with their start and end apart: 8, of which 6 were waited for; matrix products, arithmetic and copies ran while one was open for 11% of the time, Pallas kernels for 0%

profile of v1, /device:TPU:0, one launch (start us, length us, event | category | flops | bytes accessed | tf_op | source)
XLA Modules:
  0.0 126.1 jit_solution(8882846075183960452)
XLA Ops:
  0.6 3.0 %collective-permute-start = (bf16[1,1,16,1024]{3,2,1,0:T(8,128)(2,1)}, bf16[1,1,16,1024]{3,2,1,0:T(8,128)(2,1)S(1)}, u32[]{:S(2)}, u32[]{:S(2)}) collective-permute-start(bf16[1,1,16,1024]{3,2,1,0:T(8,128)(2,1)} %param.14), channel_id=1, source_target_pairs={{0,16},{16,0},{1,17},{17,1},{2,18},{18,2},{3,19},{19,3},{4,20},{20... | collective-permute-start | bytes 98312 | tf_op jit(solution)/shard_map/ppermute | solution.py:28
  3.7 0.7 iota_compare_fusion.2
  4.6 0.8 copy.45
  5.4 0.6 copy-done.3
  6.3 0.2 select_reduce_fusion
  6.7 0.8 reshape_reshape_squeeze.5
  7.7 0.8 broadcast_select_fusion.7
  8.5 2.1 %convolution_convert_fusion.1 = bf16[32,1024]{1,0:T(8,128)(2,1)S(1)} fusion(bf16[32,1024]{1,0:T(8,128)(2,1)S(1)} %bitcast.87, bf16[1024,1024]{1,0:T(8,128)(2,1)} %param.16), kind=kOutput, calls=%fused_computation.13 | convolution fusion | flops 67141632 | bytes 2228224 | tf_op jit(solution)/shard_map/dot_general | solution.py:72
  10.6 0.6 pad_maximum_fusion.2
  11.3 3.3 %all-to-all-start = ((bf16[2,1,1,16,1024]{4,3,2,1,0:T(8,128)(2,1)}), bf16[2,1,1,16,1024]{4,3,2,1,0:T(8,128)(2,1)S(1)}, u32[]{:S(2)}, u32[]{:S(2)}) async-start(bf16[2,1,1,16,1024]{4,3,2,1,0:T(8,128)(2,1)} %pad_maximum_fusion.2), calls=%async_computation | async-start | bytes 131072 | tf_op jit(solution)/shard_map/all_to_all | solution.py:75
  14.6 4.1 %all-to-all-done = bf16[2,1,1,16,1024]{4,3,2,1,0:T(8,128)(2,1)S(1)} async-done(((bf16[2,1,1,16,1024]{4,3,2,1,0:T(8,128)(2,1)}), bf16[2,1,1,16,1024]{4,3,2,1,0:T(8,128)(2,1)S(1)}, u32[]{:S(2)}, u32[]{:S(2)}) %all-to-all-start) | async-done | bytes 65568 | tf_op jit(solution)/shard_map/all_to_all | solution.py:75
  19.3 4.1 %collective-permute-done.1 = bf16[16,2048]{1,0:T(8,128)(2,1)S(1)} collective-permute-done((bf16[16,2048]{1,0:T(8,128)(2,1)S(1)}, bf16[16,2048]{1,0:T(8,128)(2,1)S(1)}, u32[]{:S(2)}, u32[]{:S(2)}) %collective-permute-start.1) | collective-permute-done | bytes 65568 | tf_op jit(solution)/shard_map/ppermute | solution.py:28
  23.5 0.6 convolution_convert_fusion
  24.1 41.9 %all_to_all.30 = bf16[16,24,2048]{2,1,0:T(8,128)(2,1)S(1)} all-to-all(bf16[16,24,2048]{2,1,0:T(8,128)(2,1)S(1)} %bitcast.77), channel_id=1, replica_groups=mesh['dp'=2,'expert'=16] {'expert'}, dimensions={0} | all-to-all | bytes 3145728 | tf_op jit(solution)/shard_map/all_to_all | solution.py:109
  66.0 1.7 %fusion.4 = f32[384,704]{0,1:T(8,128)S(1)} fusion(bf16[384,2048]{1,0:T(8,128)(2,1)S(1)} %bitcast.78, bf16[1,704,2048]{2,1,0:T(8,128)(2,1)S(1)} %copy-done.8), kind=kOutput, calls=%fused_computation.5 | convolution fusion | flops 1107296256 | bytes 5537792 | tf_op jit(solution)/shard_map/dot_general | solution.py:16
  67.8 2.5 %fusion.12 = bf16[384,704]{0,1:T(8,128)(2,1)} fusion(bf16[384,2048]{1,0:T(8,128)(2,1)S(1)} %bitcast.79, bf16[1,704,2048]{2,1,0:T(8,128)(2,1)S(1)} %copy-done.9, f32[384,704]{0,1:T(8,128)S(1)} %fusion.4), kind=kOutput, calls=%fused_computation.10 | convolution fusion | flops 1108918272 | bytes 6078464 | tf_op jit(solution)/shard_map/dot_general | solution.py:16
  70.8 2.0 %collective-permute-start.2 = (f32[32,8]{0,1:T(8,128)S(1)}, f32[32,8]{0,1:T(8,128)S(1)}, u32[]{:S(2)}, u32[]{:S(2)}) collective-permute-start(f32[32,8]{0,1:T(8,128)S(1)} %fusion.41), channel_id=1, source_target_pairs={{0,16},{16,0},{1,17},{17,1},{2,18},{18,2},{3,19},{19,3},{4,20},{20... | collective-permute-start | bytes 3080 | tf_op jit(solution)/shard_map/ppermute | solution.py:28
  72.8 12.8 %collective-permute-done.3 = bf16[384,704]{0,1:T(8,128)(2,1)} collective-permute-done((bf16[384,704]{0,1:T(8,128)(2,1)}, bf16[384,704]{0,1:T(8,128)(2,1)}, u32[]{:S(2)}, u32[]{:S(2)}) %collective-permute-start.3) | collective-permute-done | bytes 540704 | tf_op jit(solution)/shard_map/ppermute | solution.py:28
  85.7 1.3 %broadcast_select_fusion.1 = (bf16[384,704]{0,1:T(8,128)(2,1)S(1)}, bf16[384,704]{0,1:T(8,128)(2,1)S(1)}) fusion(bf16[384,704]{0,1:T(8,128)(2,1)} %fusion.12, bf16[384,704]{0,1:T(8,128)(2,1)} %collective-permute-done.3, pred[]{:T(512)S(6)} %eq.16), kind=kLoop, calls=%fused_computation.18 | loop fusion | flops 540672 | bytes 2162689 | tf_op jit(solution)/shard_map/jit(_where)/select_n | solution.py:30
  87.0 2.3 %fusion.6 = bf16[384,1024]{1,0:T(8,128)(2,1)} fusion(bf16[1,1408,1024]{2,1,0:T(8,128)(2,1)S(1)} %copy-done, bf16[384,704]{0,1:T(8,128)(2,1)S(1)} %get-tuple-element.3, bf16[384,704]{0,1:T(8,128)(2,1)S(1)} %get-tuple-element.2), kind=kOutput, calls=%fused_computation.8 | convolution fusion | flops 1109852160 | bytes 4751360 | tf_op jit(solution)/shard_map/dot_general | solution.py:119
  89.3 4.6 %all-to-all-start.2 = ((bf16[16,24,1024]{2,1,0:T(8,128)(2,1)}), bf16[16,24,1024]{2,1,0:T(8,128)(2,1)}, u32[]{:S(2)}, u32[]{:S(2)}) async-start(bf16[16,24,1024]{2,1,0:T(8,128)(2,1)} %bitcast.83), calls=%async_computation.2 | async-start | bytes 1572864 | tf_op jit(solution)/shard_map/all_to_all | solution.py:122
  93.9 2.9 %fusion.40 = f32[32,704]{1,0:T(8,128)S(1)} fusion(bf16[704,2048]{1,0:T(8,128)(2,1)} %param.24, bf16[16,2048]{1,0:T(8,128)(2,1)S(1)} %get-tuple-element.7, bf16[16,2048]{1,0:T(8,128)(2,1)S(1)} %get-tuple-element.6), kind=kOutput, calls=%fused_computation.77 | convolution fusion | flops 92536832 | bytes 3104768 | tf_op jit(solution)/shard_map/dot_general | solution.py:16
  96.8 0.9 multiply_convert_fusion.2
  97.7 0.4 collective-permute-start.4
  98.1 1.7 %gather_fusion = f32[192]{0:T(256)S(1)} fusion(f32[32,16]{0,1:T(8,128)S(1)} %pad_maximum_fusion.3, s32[192]{0:T(256)S(1)} %reshape.294), kind=kCustom, calls=%fused_computation | custom fusion | bytes 3072 | tf_op jit(solution)/shard_map/jit(take_along_axis)/gather | solution.py:83
  100.7 1.2 collective-permute-done.4
  101.9 10.8 %all-to-all-done.2 = bf16[16,24,1024]{2,1,0:T(8,128)(2,1)} async-done(((bf16[16,24,1024]{2,1,0:T(8,128)(2,1)}), bf16[16,24,1024]{2,1,0:T(8,128)(2,1)}, u32[]{:S(2)}, u32[]{:S(2)}) %all-to-all-start.2) | async-done | bytes 786464 | tf_op jit(solution)/shard_map/all_to_all | solution.py:122
  112.7 1.4 %fusion.42 = f32[32,1024]{1,0:T(8,128)S(1)} fusion(bf16[32,384]{1,0:T(8,128)(2,1)S(1)} %fusion.21, bf16[384,1024]{1,0:T(8,128)(2,1)} %bitcast.13), kind=kOutput, calls=%fused_computation.79 | convolution fusion | flops 25165824 | bytes 942080 | tf_op jit(solution)/shard_map/dot_general | solution.py:128
  114.0 3.1 %fusion.15 = f32[32,1024]{1,0:T(8,128)} fusion(f32[32,1024]{1,0:T(8,128)S(1)} %fusion.42, bf16[1408,1024]{1,0:T(8,128)(2,1)} %param.26, bf16[32,704]{1,0:T(8,128)(2,1)S(1)} %get-tuple-element.9, bf16[32,704]{1,0:T(8,128)(2,1)S(1)} %get-tuple-element.8, pred[32]{0:T(512)(128)(4,1)S(1)} %lt.57), kind=kOutput, calls=%fused_computation.12 | convolution fusion | flops 92520448 | bytes 3235872 | tf_op jit(solution)/shard_map/dot_general | solution.py:120
  117.2 3.4 %all-to-all-start.3 = ((f32[2,16,1024]{2,1,0:T(8,128)}), f32[2,16,1024]{2,1,0:T(8,128)S(1)}, u32[]{:S(2)}, u32[]{:S(2)}) async-start(f32[2,16,1024]{2,1,0:T(8,128)} %bitcast.14), calls=%async_computation.3 | async-start | bytes 262144 | tf_op jit(solution)/shard_map/all_to_all | solution.py:132
  120.7 4.3 %all-to-all-done.3 = f32[2,16,1024]{2,1,0:T(8,128)S(1)} async-done(((f32[2,16,1024]{2,1,0:T(8,128)}), f32[2,16,1024]{2,1,0:T(8,128)S(1)}, u32[]{:S(2)}, u32[]{:S(2)}) %all-to-all-start.3) | async-done | bytes 131104 | tf_op jit(solution)/shard_map/all_to_all | solution.py:132
  125.4 0.7 multiply_convert_fusion
  (71 shorter events, 3.6 us)
Async XLA Ops:
  0.6 86.4 %copy-start = (bf16[1,1408,1024]{2,1,0:T(8,128)(2,1)S(1)}, bf16[1,1408,1024]{2,1,0:T(8,128)(2,1)}, u32[]{:S(2)}) copy-start(bf16[1,1408,1024]{2,1,0:T(8,128)(2,1)} %param.23) | copy-start | bytes 8650756
  0.6 7.1 %collective-permute-start = (bf16[1,1,16,1024]{3,2,1,0:T(8,128)(2,1)}, bf16[1,1,16,1024]{3,2,1,0:T(8,128)(2,1)S(1)}, u32[]{:S(2)}, u32[]{:S(2)}) collective-permute-start(bf16[1,1,16,1024]{3,2,1,0:T(8,128)(2,1)} %param.14), channel_id=1, source_target_pairs={{0,16},{16,0},{1,17},{17,1},{2,18},{18,2},{3,19},{19,3},{4,20},{20... | collective-permute-start | bytes 98312 | tf_op jit(solution)/shard_map/ppermute | solution.py:28
  5.4 0.6 copy-start.3
  6.0 12.8 %copy-start.2 = (bf16[1,1,16,2048]{3,2,1,0:T(8,128)(2,1)S(1)}, bf16[1,1,16,2048]{3,2,1,0:T(8,128)(2,1)}, u32[]{:S(2)}) copy-start(bf16[1,1,16,2048]{3,2,1,0:T(8,128)(2,1)} %param.15) | copy-start | bytes 196612
  6.3 12.7 %copy-start.7 = (f32[2048]{0:T(1024)S(1)}, f32[2048]{0:T(1024)}, u32[]{:S(2)}) copy-start(f32[2048]{0:T(1024)} %param.17) | copy-start | bytes 24580
  11.3 7.4 %all-to-all-start = ((bf16[2,1,1,16,1024]{4,3,2,1,0:T(8,128)(2,1)}), bf16[2,1,1,16,1024]{4,3,2,1,0:T(8,128)(2,1)S(1)}, u32[]{:S(2)}, u32[]{:S(2)}) async-start(bf16[2,1,1,16,1024]{4,3,2,1,0:T(8,128)(2,1)} %pad_maximum_fusion.2), calls=%async_computation | async-start | bytes 131072 | tf_op jit(solution)/shard_map/all_to_all | solution.py:75
  19.1 4.3 %collective-permute-start.1 = (bf16[16,2048]{1,0:T(8,128)(2,1)S(1)}, bf16[16,2048]{1,0:T(8,128)(2,1)S(1)}, u32[]{:S(2)}, u32[]{:S(2)}) collective-permute-start(bf16[16,2048]{1,0:T(8,128)(2,1)S(1)} %multiply_convert_fusion.1), channel_id=1, source_target_pairs={{0,16},{16,0},{1,17},{17,1},{2,18},{18,2},{3,19},{19,3},{4,20},{20... | collective-permute-start | bytes 196616 | tf_op jit(solution)/shard_map/ppermute | solution.py:28
  23.5 42.6 %copy-start.8 = (bf16[1,704,2048]{2,1,0:T(8,128)(2,1)S(1)}, bf16[1,704,2048]{2,1,0:T(8,128)(2,1)}, u32[]{:S(2)}) copy-start(bf16[1,704,2048]{2,1,0:T(8,128)(2,1)} %param.21) | copy-start | bytes 8650756
  66.0 1.8 %copy-start.9 = (bf16[1,704,2048]{2,1,0:T(8,128)(2,1)S(1)}, bf16[1,704,2048]{2,1,0:T(8,128)(2,1)}, u32[]{:S(2)}) copy-start(bf16[1,704,2048]{2,1,0:T(8,128)(2,1)} %param.22) | copy-start | bytes 8650756
  67.8 2.5 %copy-start.5 = (s32[1,2,16,6]{2,1,3,0:T(2,128)S(1)}, s32[1,2,16,6]{2,1,3,0:T(2,128)}, u32[]{:S(2)}) copy-start(s32[1,2,16,6]{2,1,3,0:T(2,128)} %param.19) | copy-start | bytes 2308
  67.8 2.8 %copy-start.10 = (bf16[2048,8]{0,1:T(8,128)(2,1)S(1)}, bf16[2048,8]{0,1:T(8,128)(2,1)}, u32[]{:S(2)}) copy-start(bf16[2048,8]{0,1:T(8,128)(2,1)} %param.18) | copy-start | bytes 98308
  70.3 15.3 %collective-permute-start.3 = (bf16[384,704]{0,1:T(8,128)(2,1)}, bf16[384,704]{0,1:T(8,128)(2,1)}, u32[]{:S(2)}, u32[]{:S(2)}) collective-permute-start(bf16[384,704]{0,1:T(8,128)(2,1)} %fusion.12), channel_id=1, source_target_pairs={{0,16},{16,0},{1,17},{17,1},{2,18},{18,2},{3,19},{19,3},{4,20},{20... | collective-permute-start | bytes 1622024 | tf_op jit(solution)/shard_map/ppermute | solution.py:28
  70.8 27.3 %collective-permute-start.2 = (f32[32,8]{0,1:T(8,128)S(1)}, f32[32,8]{0,1:T(8,128)S(1)}, u32[]{:S(2)}, u32[]{:S(2)}) collective-permute-start(f32[32,8]{0,1:T(8,128)S(1)} %fusion.41), channel_id=1, source_target_pairs={{0,16},{16,0},{1,17},{17,1},{2,18},{18,2},{3,19},{19,3},{4,20},{20... | collective-permute-start | bytes 3080 | tf_op jit(solution)/shard_map/ppermute | solution.py:28
  89.3 23.4 %all-to-all-start.2 = ((bf16[16,24,1024]{2,1,0:T(8,128)(2,1)}), bf16[16,24,1024]{2,1,0:T(8,128)(2,1)}, u32[]{:S(2)}, u32[]{:S(2)}) async-start(bf16[16,24,1024]{2,1,0:T(8,128)(2,1)} %bitcast.83), calls=%async_computation.2 | async-start | bytes 1572864 | tf_op jit(solution)/shard_map/all_to_all | solution.py:122
  93.9 2.9 %copy-start.1 = (bf16[704,2048]{1,0:T(8,128)(2,1)S(1)}, bf16[704,2048]{1,0:T(8,128)(2,1)}, u32[]{:S(2)}) copy-start(bf16[704,2048]{1,0:T(8,128)(2,1)} %param.25) | copy-start | bytes 8650756
  97.7 4.2 %collective-permute-start.4 = (bf16[32,704]{1,0:T(8,128)(2,1)S(1)}, bf16[32,704]{1,0:T(8,128)(2,1)S(1)}, u32[]{:S(2)}, u32[]{:S(2)}) collective-permute-start(bf16[32,704]{1,0:T(8,128)(2,1)S(1)} %multiply_convert_fusion.2), channel_id=1, source_target_pairs={{0,16},{16,0},{1,17},{17,1},{2,18},{18,2},{3,19},{19,3},{4,20},{20... | collective-permute-start | bytes 135176 | tf_op jit(solution)/shard_map/ppermute | solution.py:28
  98.1 1.9 %copy-start.4 = (s32[1,2,16,6]{3,2,1,0:T(8,128)S(1)}, s32[1,2,16,6]{3,2,1,0:T(8,128)}, u32[]{:S(2)}) copy-start(s32[1,2,16,6]{3,2,1,0:T(8,128)} %copy-done.3) | copy-start | bytes 2308
  114.0 11.4 %copy-start.6 = (f32[2048]{0:T(1024)S(1)}, f32[2048]{0:T(1024)}, u32[]{:S(2)}) copy-start(f32[2048]{0:T(1024)} %param.27) | copy-start | bytes 24580
  117.2 7.8 %all-to-all-start.3 = ((f32[2,16,1024]{2,1,0:T(8,128)}), f32[2,16,1024]{2,1,0:T(8,128)S(1)}, u32[]{:S(2)}, u32[]{:S(2)}) async-start(f32[2,16,1024]{2,1,0:T(8,128)} %bitcast.14), calls=%async_computation.3 | async-start | bytes 262144 | tf_op jit(solution)/shard_map/all_to_all | solution.py:132
